TPU v7x, 256 devices: a whole 4x4x8 slice. The times are simulated.
256 devices in a mesh: ctx: 64 (over y, z_lo, x), tp: 4 (over z_hi, core).
Axes of the slice: x: 4, y: 4, z: 8 (z_hi: 2, z_lo: 4; z = z_hi * 4 + z_lo), core: 2. Of those that a mesh axis runs over, the one named last changes fastest.
Arguments:
- activations: bfloat16 [40960, 4096], P('ctx', 'tp'), may hold values from -6 to 6
- group_counts: int32 [64], replicated, may hold values from 1 to 5, as said below
- genome_starts: int32 [32], replicated, may hold values from 0 to 24448, as said below
- in_weight: bfloat16 [4096, 3, 2048], P('ctx', None, 'tp'), may hold values from -0.09375 to 0.09375
- short_taps: float32 [7, 3, 2048], P(None, None, 'tp'), may hold values from -2 to 2
- long_taps: float32 [128, 2048], P(None, 'tp'), may hold values from -0.5 to 0.5
- out_weight: bfloat16 [2048, 4096], P('tp', 'ctx'), may hold values from -0.125 to 0.125
Outputs:
- block_out: bfloat16 [40960, 4096], P('ctx', 'tp')
Inputs may be any that keep to these rules, and one draw needn't show every extreme that they name: Every device holds 1 or more blocks; group_counts[2k] + group_counts[2k+1] = 6 for every k. `genome_starts`: strictly increasing; the first entry is 0 and the last is exactly 24448.
All inputs are finite; a program needn't handle non-finite values.
Results may differ from a plain program's by a relative error of at most 0.012.
Values may be sent and summed in bfloat16 or wider, within the bound.
No kernel may reach another device: no remote copies, remote signals or barrier semaphores. Data moves between devices by JAX's collectives and lax.ppermute only.
A program may use at most 128 MiB of HBM per device.

v0:
```python
import jax
import jax.numpy as jnp
from jax import lax
from jax.sharding import PartitionSpec as P

GROUP = 128


def passed_along(shard, axis, by):
    peers = lax.axis_size(axis)
    pairs = [(i, i + by) for i in range(peers) if 0 <= i + by < peers]
    return lax.ppermute(shard, axis, pairs)


def genome_start(positions, genome_starts):
    above = genome_starts[None, :] <= positions[:, None]
    return jnp.max(jnp.where(above, genome_starts[None, :], 0), axis=1)


def causal_taps(padded, taps, positions, gstart, width):
    count = positions.shape[0]
    shape = (count,) + (1,) * (padded.ndim - 1)
    summed = jnp.zeros((count,) + padded.shape[1:], jnp.float32)
    for j in range(width):
        in_genome = (positions - j >= gstart).reshape(shape)
        window = padded[width - 1 - j : width - 1 - j + count]
        summed = summed + jnp.where(in_genome, window * taps[j], jnp.float32(0.0))
    return summed


def body(activations, group_counts, genome_starts, in_weight, short_taps, long_taps, out_weight):
    ctx_size = lax.axis_size("ctx")
    my_index = lax.axis_index("ctx")
    own_rows = activations.shape[0]
    device_ids = jnp.arange(ctx_size, dtype=jnp.int32)
    own_count = jnp.sum(jnp.where(device_ids == my_index, group_counts, 0))
    offset = jnp.sum(jnp.where(device_ids < my_index, group_counts, 0))
    row_ids = jnp.arange(own_rows, dtype=jnp.int32)
    positions = offset * GROUP + row_ids
    tail_end = own_count * GROUP

    def last_rows(source, count):
        return lax.dynamic_slice_in_dim(source, tail_end - count, count, 0)

    gstart = genome_start(positions, genome_starts)
    all_feats = lax.all_gather(activations, "tp", axis=1, tiled=True)
    widened = all_feats.astype(jnp.float32)
    normed = (
        widened * lax.rsqrt(jnp.mean(widened * widened, axis=1, keepdims=True) + 1e-06)
    ).astype(jnp.bfloat16)
    row_count = normed.shape[0]
    branches = in_weight.shape[1]
    chans = in_weight.shape[2]
    local_in = in_weight.reshape(in_weight.shape[0], branches * chans)
    both = jnp.concatenate([local_in, out_weight.T], axis=1)
    both_rows = lax.all_gather(both, "ctx", axis=0, tiled=True)
    flat = both_rows[:, : branches * chans]
    out_rows = both_rows[:, branches * chans :]
    summed = jnp.dot(normed, flat, preferred_element_type=jnp.float32)
    projected = summed.astype(jnp.bfloat16).reshape(row_count, branches, chans)
    rim_short = passed_along(last_rows(projected, 6), "ctx", 1)
    feat = causal_taps(
        jnp.concatenate([rim_short, projected], axis=0).astype(jnp.float32),
        short_taps,
        positions,
        gstart,
        7,
    )
    mixed = (feat[:, 1] * feat[:, 2]).astype(jnp.bfloat16)
    rim_long = passed_along(last_rows(mixed, 127), "ctx", 1)
    filtered = causal_taps(
        jnp.concatenate([rim_long, mixed], axis=0).astype(jnp.float32),
        long_taps,
        positions,
        gstart,
        128,
    )
    gated = (feat[:, 0] * filtered).astype(jnp.bfloat16)
    partial_out = lax.dot_general(
        gated, out_rows, (((1,), (1,)), ((), ())), preferred_element_type=jnp.float32
    )
    branch_out = lax.psum_scatter(
        partial_out.astype(jnp.bfloat16), "tp", scatter_dimension=1, tiled=True
    ).astype(jnp.float32)
    result = (activations.astype(jnp.float32) + branch_out).astype(jnp.bfloat16)
    slot_ids = jnp.arange(own_rows, dtype=jnp.int32)
    live_rows = (slot_ids < own_count * GROUP)[:, None]
    return jnp.where(live_rows, result, jnp.zeros_like(result))


def solution(mesh):
    placed = (
        P("ctx", "tp"),
        P(),
        P(),
        P("ctx", None, "tp"),
        P(None, None, "tp"),
        P(None, "tp"),
        P("tp", "ctx"),
    )
    return jax.shard_map(
        body, mesh=mesh, in_specs=placed, out_specs=P("ctx", "tp"), check_vma=False
    )
```

profile of v0, /device:TPU:1, one launch (start us, length us, event | category | flops | bytes accessed | tf_op | source)
XLA Modules:
  0.0 681.4 jit_solution(17413484477117585637)
XLA Ops:
  6.6 0.7 all-gather.3.cloned.1.call-update
  7.3 0.1 copy-done.2
  7.5 0.7 pad_maximum_fusion
  8.3 0.7 fusion.287
  10.9 1.3 add_compare_fusion.95
  12.2 79.5 %all-gather.3.cloned.1.call-done = bf16[640,4096]{1,0:T(8,128)(2,1)} async-done(((bf16[640,1024]{1,0:T(8,128)(2,1)}), bf16[640,4096]{1,0:T(8,128)(2,1)}) %all-gather.3.cloned.1.call-update) | async-done | bytes 5242896 | tf_op jit(solution)/shard_map/all_gather | solution.py:46
  91.6 3.6 fusion.2
  95.2 329.4 %all-gather.5.cloned.1.call-done = bf16[4096,2048]{1,0:T(8,128)(2,1)} async-done(((bf16[64,2048]{1,0:T(8,128)(2,1)}), bf16[4096,2048]{1,0:T(8,128)(2,1)}) %all-gather.5.cloned.1.call-update) | async-done | bytes 16777232 | tf_op jit(solution)/shard_map/all_gather | solution.py:56
  424.6 13.9 %fusion.20 = bf16[640,1536]{1,0:T(8,128)(2,1)} fusion(bf16[4096,2048]{1,0:T(8,128)(2,1)} %all-gather.5.cloned.1.call-done, bf16[640,4096]{1,0:T(8,128)(2,1)} %all-gather.3.cloned.1.call-done, f32[640]{0:T(1024)S(1)} %add_rsqrt_fusion), kind=kOutput, calls=%fused_computation.29 | convolution fusion | flops 8061911040 | bytes 19794432 | tf_op jit(solution)/shard_map/dot_general | solution.py:59
  438.5 2.8 copy.16
  441.3 0.2 constant_dynamic-slice_fusion
  441.4 2.1 collective-permute-start
  443.6 6.7 collective-permute-done
  450.3 1.0 maximum_convert_fusion
  451.4 8.1 %fusion.8 = f32[640,3,512]{0,2,1:T(8,128)S(1)} fusion(f32[646,3,512]{0,2,1:T(8,128)S(1)} %maximum_convert_fusion, f32[3,512]{1,0:T(4,128)S(1)} %get-tuple-element.270, f32[3,512]{1,0:T(4,128)S(1)} %get-tuple-element.271, f32[3,512]{1,0:T(4,128)S(1)} %get-tuple-element.272, f32[3,512]{1,0:T(4,128)S(1)} %get-tuple-element.273, ...), kind=kLoop, calls=%fused_computation.11 | loop fusion | flops 19660800 | bytes 31504768 | tf_op jit(solution)/shard_map/add | solution.py:27
  459.4 0.1 fusion.283
  459.7 4.4 collective-permute-start.1
  464.2 1.6 collective-permute-done.1
  465.8 0.4 maximum_convert_fusion.1
  466.6 15.7 %fusion.221 = f32[640,512]{0,1:T(8,128)S(1)} fusion(f32[767,512]{0,1:T(8,128)S(1)} %maximum_convert_fusion.1, f32[512]{0:T(512)S(1)} %bitcast.198, f32[512]{0:T(512)S(1)} %bitcast.180, f32[512]{0:T(512)S(1)} %bitcast.181, f32[512]{0:T(512)S(1)} %bitcast.182, f32[512]{0:T(512)S(1)} %bitcast.183, f32[512]{0:T(512)S(1)} %bitcast.184, f32[512]{0:T(512)S(1)} %bitcast.185, ...), kind=kLoop, calls=%fused_computation.325 | loop fusion | flops 31129600 | bytes 43339776 | tf_op jit(solution)/shard_map/add | solution.py:27
  482.8 47.7 %fusion.304 = bf16[640,512]{0,1:T(8,128)(2,1)S(1)} fusion(f32[767,512]{0,1:T(8,128)S(1)} %maximum_convert_fusion.1, f32[640,512]{0,1:T(8,128)S(1)} %fusion.221, f32[512]{0:T(512)S(1)} %bitcast.199, f32[512]{0:T(512)S(1)} %bitcast.200, f32[512]{0:T(512)S(1)} %bitcast.239, f32[512]{0:T(512)S(1)} %bitcast.240, f32[512]{0:T(512)S(1)} %bitcast.241, ...), kind=kLoop, calls=%fused_computation.37.clone.clone.2 | loop fusion | flops 95027200 | bytes 129363968 | tf_op jit(solution)/shard_map/dot_general | solution.py:79
  530.5 7.5 %convolution_convert_fusion = bf16[640,4096]{1,0:T(8,128)(2,1)} fusion(bf16[4096,2048]{1,0:T(8,128)(2,1)} %all-gather.5.cloned.1.call-done, bf16[640,512]{0,1:T(8,128)(2,1)S(1)} %fusion.304), kind=kOutput, calls=%fused_computation.6 | convolution fusion | flops 2686976000 | bytes 10092544 | tf_op jit(solution)/shard_map/dot_general | solution.py:79
  538.0 134.1 %reduce-scatter.2.cloned.1.call-done = bf16[640,1024]{1,0:T(8,128)(2,1)} async-done(((bf16[640,4096]{1,0:T(8,128)(2,1)}), bf16[640,1024]{1,0:T(8,128)(2,1)}) %reduce-scatter.2.cloned.1.call-update) | async-done | bytes 1310736 | tf_op jit(solution)/shard_map/reduce_scatter | solution.py:82
  672.1 2.8 fusion.25
  (117 shorter events, 1.0 us)
Async XLA Ops:
  6.6 85.1 %all-gather.3.cloned.1.call-start = ((), (), s32[]{:S(2)}) async-start(), calls=%async_computation.1 | async-start | bytes 6553600 | tf_op jit(solution)/shard_map/all_gather | solution.py:46
  7.3 417.3 %all-gather.5.cloned.1.call-start = ((), (), s32[]{:S(2)}) async-start(), calls=%async_computation.2 | async-start | bytes 17039360 | tf_op jit(solution)/shard_map/all_gather | solution.py:56
  8.2 663.8 %reduce-scatter.2.cloned.1.call-start = ((), (), s32[]{:S(2)}) async-start(), calls=%async_computation.3 | async-start | bytes 6553600 | tf_op jit(solution)/shard_map/reduce_scatter | solution.py:82
  441.4 8.9 %collective-permute-start = (bf16[6,3,512]{0,2,1:T(8,128)(2,1)S(1)}, bf16[6,3,512]{0,2,1:T(8,128)(2,1)S(1)}, u32[]{:S(2)}, u32[]{:S(2)}) collective-permute-start(bf16[6,3,512]{0,2,1:T(8,128)(2,1)S(1)} %constant_dynamic-slice_fusion), channel_id=1, source_target_pairs={{0,4},{4,8},{8,12},{12,16},{16,20},{20,24},{24,28},{28,32},{32,36}... | collective-permute-start | bytes 55304 | tf_op jit(solution)/shard_map/ppermute | solution.py:12
  459.7 6.1 collective-permute-start.1
  466.2 16.1 %copy-start.5 = (pred[640]{0:T(1024)(128)(4,1)S(1)}, pred[640]{0:T(1024)(128)(4,1)}, u32[]{:S(2)}) copy-start(pred[640]{0:T(1024)(128)(4,1)} %get-tuple-element.160) | copy-start | bytes 1924
  466.2 16.1 %copy-start.6 = (pred[640]{0:T(1024)(128)(4,1)S(1)}, pred[640]{0:T(1024)(128)(4,1)}, u32[]{:S(2)}) copy-start(pred[640]{0:T(1024)(128)(4,1)} %get-tuple-element.161) | copy-start | bytes 1924
  466.2 16.1 %copy-start.7 = (pred[640]{0:T(1024)(128)(4,1)S(1)}, pred[640]{0:T(1024)(128)(4,1)}, u32[]{:S(2)}) copy-start(pred[640]{0:T(1024)(128)(4,1)} %get-tuple-element.162) | copy-start | bytes 1924
  466.2 16.1 %copy-start.8 = (pred[640]{0:T(1024)(128)(4,1)S(1)}, pred[640]{0:T(1024)(128)(4,1)}, u32[]{:S(2)}) copy-start(pred[640]{0:T(1024)(128)(4,1)} %get-tuple-element.163) | copy-start | bytes 1924
  466.3 16.1 %copy-start.9 = (pred[640]{0:T(1024)(128)(4,1)S(1)}, pred[640]{0:T(1024)(128)(4,1)}, u32[]{:S(2)}) copy-start(pred[640]{0:T(1024)(128)(4,1)} %get-tuple-element.164) | copy-start | bytes 1924
  466.3 16.1 %copy-start.10 = (pred[640]{0:T(1024)(128)(4,1)S(1)}, pred[640]{0:T(1024)(128)(4,1)}, u32[]{:S(2)}) copy-start(pred[640]{0:T(1024)(128)(4,1)} %get-tuple-element.165) | copy-start | bytes 1924
  466.3 16.1 %copy-start.11 = (pred[640]{0:T(1024)(128)(4,1)S(1)}, pred[640]{0:T(1024)(128)(4,1)}, u32[]{:S(2)}) copy-start(pred[640]{0:T(1024)(128)(4,1)} %get-tuple-element.166) | copy-start | bytes 1924
  466.3 16.1 %copy-start.12 = (pred[640]{0:T(1024)(128)(4,1)S(1)}, pred[640]{0:T(1024)(128)(4,1)}, u32[]{:S(2)}) copy-start(pred[640]{0:T(1024)(128)(4,1)} %get-tuple-element.167) | copy-start | bytes 1924
  466.3 16.1 %copy-start.13 = (pred[640]{0:T(1024)(128)(4,1)S(1)}, pred[640]{0:T(1024)(128)(4,1)}, u32[]{:S(2)}) copy-start(pred[640]{0:T(1024)(128)(4,1)} %get-tuple-element.168) | copy-start | bytes 1924
  466.3 16.1 %copy-start.14 = (pred[640]{0:T(1024)(128)(4,1)S(1)}, pred[640]{0:T(1024)(128)(4,1)}, u32[]{:S(2)}) copy-start(pred[640]{0:T(1024)(128)(4,1)} %get-tuple-element.169) | copy-start | bytes 1924
  466.3 16.1 %copy-start.15 = (pred[640]{0:T(1024)(128)(4,1)S(1)}, pred[640]{0:T(1024)(128)(4,1)}, u32[]{:S(2)}) copy-start(pred[640]{0:T(1024)(128)(4,1)} %get-tuple-element.170) | copy-start | bytes 1924
  466.3 16.1 %copy-start.16 = (pred[640]{0:T(1024)(128)(4,1)S(1)}, pred[640]{0:T(1024)(128)(4,1)}, u32[]{:S(2)}) copy-start(pred[640]{0:T(1024)(128)(4,1)} %get-tuple-element.171) | copy-start | bytes 1924
  466.3 16.1 %copy-start.17 = (pred[640]{0:T(1024)(128)(4,1)S(1)}, pred[640]{0:T(1024)(128)(4,1)}, u32[]{:S(2)}) copy-start(pred[640]{0:T(1024)(128)(4,1)} %get-tuple-element.172) | copy-start | bytes 1924
  466.3 16.1 %copy-start.18 = (pred[640]{0:T(1024)(128)(4,1)S(1)}, pred[640]{0:T(1024)(128)(4,1)}, u32[]{:S(2)}) copy-start(pred[640]{0:T(1024)(128)(4,1)} %get-tuple-element.173) | copy-start | bytes 1924
  466.4 16.1 %copy-start.19 = (pred[640]{0:T(1024)(128)(4,1)S(1)}, pred[640]{0:T(1024)(128)(4,1)}, u32[]{:S(2)}) copy-start(pred[640]{0:T(1024)(128)(4,1)} %get-tuple-element.174) | copy-start | bytes 1924
  466.4 16.1 %copy-start.20 = (pred[640]{0:T(1024)(128)(4,1)S(1)}, pred[640]{0:T(1024)(128)(4,1)}, u32[]{:S(2)}) copy-start(pred[640]{0:T(1024)(128)(4,1)} %get-tuple-element.175) | copy-start | bytes 1924
  466.4 16.1 %copy-start.21 = (pred[640]{0:T(1024)(128)(4,1)S(1)}, pred[640]{0:T(1024)(128)(4,1)}, u32[]{:S(2)}) copy-start(pred[640]{0:T(1024)(128)(4,1)} %get-tuple-element.176) | copy-start | bytes 1924
  466.4 16.1 %copy-start.22 = (pred[640]{0:T(1024)(128)(4,1)S(1)}, pred[640]{0:T(1024)(128)(4,1)}, u32[]{:S(2)}) copy-start(pred[640]{0:T(1024)(128)(4,1)} %get-tuple-element.177) | copy-start | bytes 1924
  538.0 134.1 %copy-start = (bf16[640,1024]{1,0:T(8,128)(2,1)S(1)}, bf16[640,1024]{1,0:T(8,128)(2,1)}, u32[]{:S(2)}) copy-start(bf16[640,1024]{1,0:T(8,128)(2,1)} %param.7) | copy-start | bytes 3932164
  (28 other events, 370.7 us)
Sparse Core Ops, SparseCore 0:
  9.2 82.4 all-gather.2
  93.4 331.1 all-gather.4
  538.1 133.9 reduce-scatter.1
where the time goes:
time: 682 us; the launch traced here: 681 us
  waiting for transfers between devices  552 us (81%)
  other arithmetic  82.4 us (12%)
  matrix products  21.3 us (3%)
  between operations  15.4 us (2%)
    all_gather x1, waiting for transfers between devices, body(): both_rows = lax.all_gather(both, 'ctx', axis=0, tiled=True)  329 us
    reduce_scatter x1, waiting for transfers between devices, body(): lax.psum_scatter(partial_out.astype(jnp.bfloat16), 'tp', scatter_dimensio...  134 us
    all_gather x1, waiting for transfers between devices, body(): all_feats = lax.all_gather(activations, 'tp', axis=1, tiled=True)  79.5 us
    dot_general x1, other arithmetic, body(): lax.dot_general(gated, out_rows, (((1,), (1,)), ((), ())), preferred_elem...  47.7 us
    add x2, other arithmetic, causal_taps(): summed = summed + jnp.where(in_genome, window * taps[j], jnp.float32(0.0))  23.8 us
    dot_general x1, matrix products, body(): summed = jnp.dot(normed, flat, preferred_element_type=jnp.float32)  13.9 us
  transfers between devices with their start and end apart: 5, of which 5 were waited for; matrix products, arithmetic and copies ran while one was open for 1% of the time, Pallas kernels for 0%

commit v1 on v0

--- a/solution.py
+++ b/solution.py
@@ -43,7 +43,9 @@
         return lax.dynamic_slice_in_dim(source, tail_end - count, count, 0)
 
     gstart = genome_start(positions, genome_starts)
-    all_feats = lax.all_gather(activations, "tp", axis=1, tiled=True)
+    all_feats = jnp.concatenate(
+        lax.all_to_all(jnp.stack([activations] * lax.axis_size("tp")), "tp", 0, 0), axis=1
+    )
     widened = all_feats.astype(jnp.float32)
     normed = (
         widened * lax.rsqrt(jnp.mean(widened * widened, axis=1, keepdims=True) + 1e-06)

time: 682 us -> 668 us (0.979)
  waiting for transfers between devices: 552 us -> 517 us
  starting transfers between devices: 6.61 us -> 15.7 us
    all_to_all x0 -> x1, waiting for transfers between devices: none -> 167 us  [body(): lax.all_to_all(jnp.stack([activations] * lax.axis_size('tp')), 'tp', 0, 0)]
    all_gather x1, waiting for transfers between devices: 329 us -> 216 us  [body(): both_rows = lax.all_gather(both, 'ctx', axis=0, tiled=True)]
    all_gather x1 -> x0, waiting for transfers between devices: 79.5 us -> none  [body(): all_feats = lax.all_gather(activations, 'tp', axis=1, tiled=True)]
    all_to_all x0 -> x1, starting transfers between devices: none -> 10.1 us  [body(): lax.all_to_all(jnp.stack([activations] * lax.axis_size('tp')), 'tp', 0, 0)]
    reduce_scatter x1, waiting for transfers between devices: 134 us -> 126 us  [body(): lax.psum_scatter(partial_out.astype(jnp.bfloat16), 'tp', scatter_dimensio...]
  transfers between devices with their start and end apart: 5 -> 5, of which waited for: 5 -> 5; matrix products, arithmetic and copies ran while one was open for 1% -> 2% of each run, Pallas kernels for 0% -> 0%
where the time goes in v1:
time: 668 us
  waiting for transfers between devices  517 us (77%)
  other arithmetic  89.2 us (13%)
  matrix products  21.5 us (3%)
  starting transfers between devices  15.7 us (2%)
  between operations  15.6 us (2%)
  local copies, waits for them, and re-layouts  8.96 us (1%)
    all_gather x1, waiting for transfers between devices, body(): both_rows = lax.all_gather(both, 'ctx', axis=0, tiled=True)  216 us
    all_to_all x1, waiting for transfers between devices, body(): lax.all_to_all(jnp.stack([activations] * lax.axis_size('tp')), 'tp', 0, 0)  167 us
    reduce_scatter x1, waiting for transfers between devices, body(): lax.psum_scatter(partial_out.astype(jnp.bfloat16), 'tp', scatter_dimensio...  126 us
    dot_general x1, other arithmetic, body(): lax.dot_general(gated, out_rows, (((1,), (1,)), ((), ())), preferred_elem...  47.7 us
    add x2, other arithmetic, causal_taps(): summed = summed + jnp.where(in_genome, window * taps[j], jnp.float32(0.0))  23.8 us
    dot_general x1, matrix products, body(): summed = jnp.dot(normed, flat, preferred_element_type=jnp.float32)  14 us
  transfers between devices with their start and end apart: 5, of which 5 were waited for; matrix products, arithmetic and copies ran while one was open for 2% of the time, Pallas kernels for 0%

profile of v1, /device:TPU:1, one launch (start us, length us, event | category | flops | bytes accessed | tf_op | source)
XLA Modules:
  0.0 667.9 jit_solution(15426177450977528421)
XLA Ops:
  6.5 0.9 copy.32
  7.5 1.6 pad_maximum_fusion
  9.1 1.7 copy.16
  10.8 2.8 stack.2
  13.6 10.1 %all-to-all-start = ((bf16[4,640,1024]{1,2,0:T(8,128)(2,1)}), bf16[4,640,1024]{1,2,0:T(8,128)(2,1)}, u32[]{:S(2)}, u32[]{:S(2)}) async-start(bf16[4,640,1024]{1,2,0:T(8,128)(2,1)} %stack.2), calls=%async_computation | async-start | bytes 10485760 | tf_op jit(solution)/shard_map/all_to_all | solution.py:47
  23.7 0.7 fusion.282
  26.2 1.3 add_compare_fusion.95
  27.5 166.9 %all-to-all-done = bf16[4,640,1024]{1,2,0:T(8,128)(2,1)} async-done(((bf16[4,640,1024]{1,2,0:T(8,128)(2,1)}), bf16[4,640,1024]{1,2,0:T(8,128)(2,1)}, u32[]{:S(2)}, u32[]{:S(2)}) %all-to-all-start) | async-done | bytes 5242912 | tf_op jit(solution)/shard_map/all_to_all | solution.py:47
  194.4 3.6 multiply_reduce_fusion
  198.0 6.0 fusion.2
  204.0 216.5 %all-gather.2.cloned.1.call-done = bf16[4096,2048]{1,0:T(8,128)(2,1)} async-done(((bf16[64,2048]{1,0:T(8,128)(2,1)}), bf16[4096,2048]{1,0:T(8,128)(2,1)}) %all-gather.2.cloned.1.call-update) | async-done | bytes 16777232 | tf_op jit(solution)/shard_map/all_gather | solution.py:58
  420.4 14.0 %fusion.17 = bf16[640,1536]{1,0:T(8,128)(2,1)} fusion(bf16[640,4096]{0,1:T(8,128)(2,1)} %fusion.2, bf16[4096,2048]{1,0:T(8,128)(2,1)} %all-gather.2.cloned.1.call-done), kind=kOutput, calls=%fused_computation.27 | convolution fusion | flops 8054046720 | bytes 19791872 | tf_op jit(solution)/shard_map/dot_general | solution.py:61
  434.4 2.8 copy.18
  437.4 1.3 collective-permute-start
  438.8 6.2 collective-permute-done
  445.0 1.0 maximum_convert_fusion
  446.0 8.1 %fusion.5 = f32[640,3,512]{0,2,1:T(8,128)S(1)} fusion(f32[646,3,512]{0,2,1:T(8,128)S(1)} %maximum_convert_fusion, f32[3,512]{1,0:T(4,128)S(1)} %get-tuple-element.270, f32[3,512]{1,0:T(4,128)S(1)} %get-tuple-element.271, f32[3,512]{1,0:T(4,128)S(1)} %get-tuple-element.272, f32[3,512]{1,0:T(4,128)S(1)} %get-tuple-element.273, ...), kind=kLoop, calls=%fused_computation.9 | loop fusion | flops 19660800 | bytes 31504768 | tf_op jit(solution)/shard_map/add | solution.py:27
  454.3 4.2 collective-permute-start.1
  458.7 1.6 collective-permute-done.1
  461.1 15.7 %fusion.216 = f32[640,512]{0,1:T(8,128)S(1)} fusion(f32[767,512]{0,1:T(8,128)S(1)} %maximum_convert_fusion.1, f32[512]{0:T(512)S(1)} %bitcast.205, f32[512]{0:T(512)S(1)} %bitcast.187, f32[512]{0:T(512)S(1)} %bitcast.188, f32[512]{0:T(512)S(1)} %bitcast.189, f32[512]{0:T(512)S(1)} %bitcast.190, f32[512]{0:T(512)S(1)} %bitcast.191, f32[512]{0:T(512)S(1)} %bitcast.192, ...), kind=kLoop, calls=%fused_computation.323 | loop fusion | flops 31129600 | bytes 43339776 | tf_op jit(solution)/shard_map/add | solution.py:27
  477.2 47.7 %fusion.300 = bf16[640,512]{0,1:T(8,128)(2,1)S(1)} fusion(f32[767,512]{0,1:T(8,128)S(1)} %maximum_convert_fusion.1, f32[640,512]{0,1:T(8,128)S(1)} %fusion.216, f32[512]{0:T(512)S(1)} %bitcast.206, f32[512]{0:T(512)S(1)} %bitcast.207, f32[512]{0:T(512)S(1)} %bitcast.246, f32[512]{0:T(512)S(1)} %bitcast.247, f32[512]{0:T(512)S(1)} %bitcast.248, ...), kind=kLoop, calls=%fused_computation.35.clone.clone.2 | loop fusion | flops 95027200 | bytes 129363968 | tf_op jit(solution)/shard_map/dot_general | solution.py:81
  524.9 7.5 %convolution_convert_fusion = bf16[640,4096]{1,0:T(8,128)(2,1)} fusion(bf16[4096,2048]{1,0:T(8,128)(2,1)} %all-gather.2.cloned.1.call-done, bf16[640,512]{0,1:T(8,128)(2,1)S(1)} %fusion.300), kind=kOutput, calls=%fused_computation.5 | convolution fusion | flops 2686976000 | bytes 10092544 | tf_op jit(solution)/shard_map/dot_general | solution.py:81
  532.5 125.8 %reduce-scatter.2.cloned.1.call-done = bf16[640,1024]{1,0:T(8,128)(2,1)} async-done(((bf16[640,4096]{1,0:T(8,128)(2,1)}), bf16[640,1024]{1,0:T(8,128)(2,1)}) %reduce-scatter.2.cloned.1.call-update) | async-done | bytes 1310736 | tf_op jit(solution)/shard_map/reduce_scatter | solution.py:84
  658.3 2.8 fusion.20
  (115 shorter events, 1.5 us)
Async XLA Ops:
  6.5 413.9 %all-gather.2.cloned.1.call-start = ((), (), s32[]{:S(2)}) async-start(), calls=%async_computation.2 | async-start | bytes 17039360 | tf_op jit(solution)/shard_map/all_gather | solution.py:58
  13.6 180.8 %all-to-all-start = ((bf16[4,640,1024]{1,2,0:T(8,128)(2,1)}), bf16[4,640,1024]{1,2,0:T(8,128)(2,1)}, u32[]{:S(2)}, u32[]{:S(2)}) async-start(bf16[4,640,1024]{1,2,0:T(8,128)(2,1)} %stack.2), calls=%async_computation | async-start | bytes 10485760 | tf_op jit(solution)/shard_map/all_to_all | solution.py:47
  23.7 634.6 %reduce-scatter.2.cloned.1.call-start = ((), (), s32[]{:S(2)}) async-start(), calls=%async_computation.3 | async-start | bytes 6553600 | tf_op jit(solution)/shard_map/reduce_scatter | solution.py:84
  437.4 7.5 %collective-permute-start = (bf16[6,3,512]{0,2,1:T(8,128)(2,1)S(1)}, bf16[6,3,512]{0,2,1:T(8,128)(2,1)S(1)}, u32[]{:S(2)}, u32[]{:S(2)}) collective-permute-start(bf16[6,3,512]{0,2,1:T(8,128)(2,1)S(1)} %constant_dynamic-slice_fusion), channel_id=1, source_target_pairs={{0,4},{4,8},{8,12},{12,16},{16,20},{20,24},{24,28},{28,32},{32,36}... | collective-permute-start | bytes 55304 | tf_op jit(solution)/shard_map/ppermute | solution.py:12
  454.3 6.0 collective-permute-start.1
  460.7 16.1 %copy-start.3 = (pred[640]{0:T(1024)(128)(4,1)S(1)}, pred[640]{0:T(1024)(128)(4,1)}, u32[]{:S(2)}) copy-start(pred[640]{0:T(1024)(128)(4,1)} %get-tuple-element.160) | copy-start | bytes 1924
  460.7 16.1 %copy-start.4 = (pred[640]{0:T(1024)(128)(4,1)S(1)}, pred[640]{0:T(1024)(128)(4,1)}, u32[]{:S(2)}) copy-start(pred[640]{0:T(1024)(128)(4,1)} %get-tuple-element.161) | copy-start | bytes 1924
  460.7 16.1 %copy-start.5 = (pred[640]{0:T(1024)(128)(4,1)S(1)}, pred[640]{0:T(1024)(128)(4,1)}, u32[]{:S(2)}) copy-start(pred[640]{0:T(1024)(128)(4,1)} %get-tuple-element.162) | copy-start | bytes 1924
  460.7 16.1 %copy-start.6 = (pred[640]{0:T(1024)(128)(4,1)S(1)}, pred[640]{0:T(1024)(128)(4,1)}, u32[]{:S(2)}) copy-start(pred[640]{0:T(1024)(128)(4,1)} %get-tuple-element.163) | copy-start | bytes 1924
  460.7 16.1 %copy-start.7 = (pred[640]{0:T(1024)(128)(4,1)S(1)}, pred[640]{0:T(1024)(128)(4,1)}, u32[]{:S(2)}) copy-start(pred[640]{0:T(1024)(128)(4,1)} %get-tuple-element.164) | copy-start | bytes 1924
  460.7 16.1 %copy-start.8 = (pred[640]{0:T(1024)(128)(4,1)S(1)}, pred[640]{0:T(1024)(128)(4,1)}, u32[]{:S(2)}) copy-start(pred[640]{0:T(1024)(128)(4,1)} %get-tuple-element.165) | copy-start | bytes 1924
  460.7 16.1 %copy-start.9 = (pred[640]{0:T(1024)(128)(4,1)S(1)}, pred[640]{0:T(1024)(128)(4,1)}, u32[]{:S(2)}) copy-start(pred[640]{0:T(1024)(128)(4,1)} %get-tuple-element.166) | copy-start | bytes 1924
  460.8 16.1 %copy-start.10 = (pred[640]{0:T(1024)(128)(4,1)S(1)}, pred[640]{0:T(1024)(128)(4,1)}, u32[]{:S(2)}) copy-start(pred[640]{0:T(1024)(128)(4,1)} %get-tuple-element.167) | copy-start | bytes 1924
  460.8 16.1 %copy-start.11 = (pred[640]{0:T(1024)(128)(4,1)S(1)}, pred[640]{0:T(1024)(128)(4,1)}, u32[]{:S(2)}) copy-start(pred[640]{0:T(1024)(128)(4,1)} %get-tuple-element.168) | copy-start | bytes 1924
  460.8 16.1 %copy-start.12 = (pred[640]{0:T(1024)(128)(4,1)S(1)}, pred[640]{0:T(1024)(128)(4,1)}, u32[]{:S(2)}) copy-start(pred[640]{0:T(1024)(128)(4,1)} %get-tuple-element.169) | copy-start | bytes 1924
  460.8 16.1 %copy-start.13 = (pred[640]{0:T(1024)(128)(4,1)S(1)}, pred[640]{0:T(1024)(128)(4,1)}, u32[]{:S(2)}) copy-start(pred[640]{0:T(1024)(128)(4,1)} %get-tuple-element.170) | copy-start | bytes 1924
  460.8 16.1 %copy-start.14 = (pred[640]{0:T(1024)(128)(4,1)S(1)}, pred[640]{0:T(1024)(128)(4,1)}, u32[]{:S(2)}) copy-start(pred[640]{0:T(1024)(128)(4,1)} %get-tuple-element.171) | copy-start | bytes 1924
  460.8 16.1 %copy-start.15 = (pred[640]{0:T(1024)(128)(4,1)S(1)}, pred[640]{0:T(1024)(128)(4,1)}, u32[]{:S(2)}) copy-start(pred[640]{0:T(1024)(128)(4,1)} %get-tuple-element.172) | copy-start | bytes 1924
  460.8 16.1 %copy-start.16 = (pred[640]{0:T(1024)(128)(4,1)S(1)}, pred[640]{0:T(1024)(128)(4,1)}, u32[]{:S(2)}) copy-start(pred[640]{0:T(1024)(128)(4,1)} %get-tuple-element.173) | copy-start | bytes 1924
  460.8 16.1 %copy-start.17 = (pred[640]{0:T(1024)(128)(4,1)S(1)}, pred[640]{0:T(1024)(128)(4,1)}, u32[]{:S(2)}) copy-start(pred[640]{0:T(1024)(128)(4,1)} %get-tuple-element.174) | copy-start | bytes 1924
  460.8 16.1 %copy-start.18 = (pred[640]{0:T(1024)(128)(4,1)S(1)}, pred[640]{0:T(1024)(128)(4,1)}, u32[]{:S(2)}) copy-start(pred[640]{0:T(1024)(128)(4,1)} %get-tuple-element.175) | copy-start | bytes 1924
  460.8 16.1 %copy-start.19 = (pred[640]{0:T(1024)(128)(4,1)S(1)}, pred[640]{0:T(1024)(128)(4,1)}, u32[]{:S(2)}) copy-start(pred[640]{0:T(1024)(128)(4,1)} %get-tuple-element.176) | copy-start | bytes 1924
  460.9 16.1 %copy-start.20 = (pred[640]{0:T(1024)(128)(4,1)S(1)}, pred[640]{0:T(1024)(128)(4,1)}, u32[]{:S(2)}) copy-start(pred[640]{0:T(1024)(128)(4,1)} %get-tuple-element.177) | copy-start | bytes 1924
  532.4 125.8 %copy-start = (bf16[640,1024]{1,0:T(8,128)(2,1)S(1)}, bf16[640,1024]{1,0:T(8,128)(2,1)}, u32[]{:S(2)}) copy-start(bf16[640,1024]{1,0:T(8,128)(2,1)} %param.7) | copy-start | bytes 3932164
  (26 other events, 401.9 us)
Sparse Core Ops, SparseCore 0:
  9.2 411.1 all-gather.1
  532.6 125.6 reduce-scatter.1
